TPU v7x, 32 devices: a whole 2x2x4 slice. The times are simulated.
32 devices in a mesh: dp: 8 (over y, x, core), tensor: 4 (over z).
Axes of the slice: x: 2, y: 2, z: 4, core: 2. Of those that a mesh axis runs over, the one named last changes fastest.
Arguments:
- teacher_master: float32 [256, 16384], P('dp', 'tensor'), as said below
- student_weight: bfloat16 [256, 16384], P('dp', 'tensor'), may hold values from -6 to 6
- teacher_feat: bfloat16 [2048, 256], P('dp'), as said below
- student_feat: bfloat16 [2048, 256], P('dp'), may hold values from -6 to 6
- center: float32 [16384], P('tensor'), may hold values from -0.3 to 0.3
Outputs:
- master_new: float32 [256, 16384], P('dp', 'tensor')
- student_grad: float32 [256, 16384], P('dp', 'tensor')
- new_center: float32 [16384], P('tensor')
Inputs may be any that keep to these rules, and one draw needn't show every extreme that they name: `teacher_feat`: rows of teacher features are real-valued and of order one. `teacher_master`: entries of the teacher master are real-valued and of order one.
All inputs are finite; a program needn't handle non-finite values.
Results may differ from a plain program's by a relative error of at most 0.014.
Values may be sent and summed in bfloat16 or wider, within the bound.
No kernel may reach another device: no remote copies, remote signals or barrier semaphores. Data moves between devices by JAX's collectives and lax.ppermute only.
A program may use at most 64 MiB of HBM per device.

v0:
```python
import jax
import jax.numpy as jnp
from jax import lax
from jax.sharding import PartitionSpec as P


def unit_rows(feat):
    wide = feat.astype(jnp.float32)
    return (wide * lax.rsqrt(jnp.sum(wide * wide, 1, keepdims=True) + 1e-06)).astype(jnp.bfloat16)


def shards(teacher_master, student_weight, teacher_feat, student_feat, center):
    zt = unit_rows(teacher_feat)
    zs = unit_rows(student_feat)
    images_all = teacher_feat.shape[0] * lax.axis_size("dp")
    student_full = lax.all_gather(student_weight, "dp", axis=0, tiled=True)
    master_new = 0.996 * teacher_master + 0.004 * student_weight.astype(jnp.float32)
    weight = lax.all_gather(master_new.astype(jnp.bfloat16), "dp", axis=0, tiled=True)
    feats = zt
    raw = jnp.dot(feats, weight, preferred_element_type=jnp.float32)
    squares = jnp.sum(jnp.square(weight.astype(jnp.float32)), 0)
    t_norm = jnp.sqrt(squares + 1e-06)
    t_cos = raw / t_norm
    s_norm = jnp.sqrt(jnp.sum(jnp.square(student_full.astype(jnp.float32)), 0) + 1e-06)
    s_cos = jnp.dot(zs, student_full, preferred_element_type=jnp.float32) / s_norm
    t_exp = jnp.exp((t_cos - center) / 0.04)
    s_exp = jnp.exp(s_cos / 0.1)
    t_total, s_total = lax.psum(
        (jnp.sum(t_exp, 1, keepdims=True), jnp.sum(s_exp, 1, keepdims=True)), "tensor"
    )
    cos_mean = lax.psum(jnp.sum(t_cos, 0), "dp") / images_all
    new_center = 0.5 * center + 0.5 * cos_mean
    dlog = ((s_exp / s_total - t_exp / t_total) / 0.1).astype(jnp.bfloat16)
    weighted = jnp.sum(dlog.astype(jnp.float32) * s_cos, 0)
    scaled = weighted / s_norm
    feats = zs
    product = lax.dot_general(
        feats, dlog, (((0,), (0,)), ((), ())), preferred_element_type=jnp.float32
    )
    student_grad = lax.psum_scatter(
        (product - student_full.astype(jnp.float32) * scaled) / s_norm,
        "dp",
        scatter_dimension=0,
        tiled=True,
    )
    return (master_new, student_grad, new_center)


def solution(mesh):
    placed = (P("dp", "tensor"), P("dp", "tensor"), P("dp", None), P("dp", None), P("tensor"))
    return jax.shard_map(
        shards,
        mesh=mesh,
        in_specs=placed,
        out_specs=(P("dp", "tensor"), P("dp", "tensor"), P("tensor")),
        check_vma=False,
    )
```

profile of v0, /device:TPU:0, one launch (start us, length us, event | category | flops | bytes accessed | tf_op | source)
XLA Modules:
  0.0 153.8 jit_solution(11268141412257356897)
XLA Ops:
  7.2 0.0 copy-start.3
  7.2 0.0 all-gather.3.cloned.1.call-start
  7.2 0.7 all-gather.3.cloned.1.call-update
  7.9 0.0 all-gather.5.cloned.1.call-start
  8.0 2.1 %fusion.13 = (bf16[32,4096]{1,0:T(8,128)(2,1)}, f32[32,4096]{1,0:T(8,128)}) fusion(bf16[32,4096]{1,0:T(8,128)(2,1)} %param.6, f32[32,4096]{1,0:T(8,128)} %param.5), kind=kLoop, calls=%fused_computation.31 | loop fusion | flops 655360 | bytes 1572864 | tf_op jit(solution)/shard_map/convert_element_type | solution.py:18
  10.0 0.0 all-gather.5.cloned.1.call-update
  10.1 0.0 reduce-scatter.2.cloned.1.call-start
  10.1 1.0 fusion.6
  11.1 1.0 fusion.4
  12.2 28.3 %all-gather.3.cloned.1.call-done = bf16[256,4096]{1,0:T(8,128)(2,1)} async-done(((bf16[32,4096]{1,0:T(8,128)(2,1)}), bf16[256,4096]{1,0:T(8,128)(2,1)}) %all-gather.3.cloned.1.call-update) | async-done | bytes 2097168 | tf_op jit(solution)/shard_map/all_gather | solution.py:16
  40.5 0.0 copy-start
  40.5 2.2 %fusion.1 = f32[4096]{0:T(1024)S(1)} fusion(bf16[256,4096]{1,0:T(8,128)(2,1)} %all-gather.3.cloned.1.call-done), kind=kLoop, calls=%fused_computation.6 | loop fusion | flops 3141632 | bytes 2113536 | tf_op jit(solution)/shard_map/reduce_sum | solution.py:24
  42.7 28.2 %all-gather.5.cloned.1.call-done = bf16[256,4096]{1,0:T(8,128)(2,1)} async-done(((bf16[32,4096]{1,0:T(8,128)(2,1)}), bf16[256,4096]{1,0:T(8,128)(2,1)}) %all-gather.5.cloned.1.call-update) | async-done | bytes 2097168 | tf_op jit(solution)/shard_map/all_gather | solution.py:18
  70.9 2.0 %multiply_reduce_fusion.1 = f32[4096]{0:T(1024)S(1)} fusion(bf16[256,4096]{1,0:T(8,128)(2,1)} %all-gather.5.cloned.1.call-done), kind=kLoop, calls=%fused_computation.10 | loop fusion | flops 3141632 | bytes 2113536 | tf_op jit(solution)/shard_map/reduce_sum | solution.py:21
  73.0 0.0 copy-done.3
  73.0 0.0 copy-done
  73.0 0.0 copy-start.1
  73.0 0.0 copy-start.2
  73.0 0.0 copy-start.4
  73.0 3.1 %fusion.2 = (f32[256]{0:T(256)S(1)}, f32[256,4096]{1,0:T(8,128)}) fusion(f32[4096]{0:T(1024)S(1)} %add_sqrt_fusion.1, bf16[256,4096]{1,0:T(8,128)(2,1)S(1)} %copy-done, bf16[256,256]{1,0:T(8,128)(2,1)S(1)} %copy-done.3, f32[256]{0:T(256)S(1)} %add_rsqrt_fusion.1), kind=kOutput, calls=%fused_computation.12 | convolution fusion | flops 540212992 | bytes 6440960 | tf_op jit(solution)/shard_map/dot_general | solution.py:25
  76.1 0.0 copy-done.1
  76.1 0.0 copy-done.2
  76.1 0.0 copy-done.4
  76.1 3.4 %fusion.12 = (f32[4096]{0:T(1024)S(1)}, f32[256]{0:T(256)S(1)}, f32[256,4096]{1,0:T(8,128)}) fusion(f32[4096]{0:T(1024)S(1)} %copy-done.4, f32[4096]{0:T(1024)S(1)} %add_sqrt_fusion, bf16[256,4096]{1,0:T(8,128)(2,1)S(1)} %copy-done.1, bf16[256,256]{1,0:T(8,128)(2,1)S(1)} %copy-done.2, f32[256]{0:T(256)S(1)} %add_rsqrt_fusion), kind=kOutput, calls=%fused_computation.30 | convolution fusion | flops 542306048 | bytes 6473728 | tf_op jit(solution)/shard_map/dot_general | solution.py:20
  79.5 11.7 %all-reduce = (f32[256]{0:T(256)S(1)}, f32[256]{0:T(256)S(1)}) all-reduce(f32[256]{0:T(256)S(1)} %get-tuple-element.4, f32[256]{0:T(256)S(1)} %get-tuple-element.12), channel_id=1, replica_groups=mesh['dp'=8,'tensor'=4] {'tensor'}, use_global_device_ids=true, to_apply=%region_7.0 | all-reduce | flops 512 | bytes 4096 | tf_op jit(solution)/shard_map/psum | solution.py:28
  91.1 4.5 %multiply_reduce_fusion = (f32[4096]{0:T(1024)S(1)}, bf16[256,4096]{1,0:T(8,128)(2,1)S(1)}) fusion(f32[256,4096]{1,0:T(8,128)} %get-tuple-element.13, f32[256]{0:T(256)S(1)} %get-tuple-element.5, f32[256,4096]{1,0:T(8,128)} %get-tuple-element.11, f32[4096]{0:T(1024)S(1)} %copy-done.4, f32[256]{0:T(256)S(1)} %get-tuple-element.6), kind=kLoop, calls=%fused_computation.7 | loop fusion | flops 11530240 | bytes 10520576 | tf_op jit(solution)/shard_map/reduce_sum | solution.py:34
  95.6 3.0 %fusion = f32[256,4096]{1,0:T(8,128)} fusion(bf16[256,4096]{1,0:T(8,128)(2,1)S(1)} %get-tuple-element.8, bf16[256,4096]{1,0:T(8,128)(2,1)S(1)} %copy-done, f32[4096]{0:T(1024)S(1)} %rsqrt_multiply_fusion, f32[4096]{0:T(1024)S(1)} %add_sqrt_fusion.1, bf16[256,256]{1,0:T(8,128)(2,1)S(1)} %copy-done.3, f32[256]{0:T(256)S(1)} %add_rsqrt_fusion.1), kind=kOutput, calls=%fused_computation.5 | convolution fusion | flops 541261824 | bytes 8553472 | tf_op jit(solution)/shard_map/dot_general | solution.py:37
  98.6 0.0 reduce-scatter.2.cloned.1.call-update
  98.6 22.4 %psum.23 = f32[4096]{0:T(1024)S(1)} all-reduce(f32[4096]{0:T(1024)S(1)} %get-tuple-element.3), channel_id=1, replica_groups=mesh['dp'=8,'tensor'=4] {'dp'}, use_global_device_ids=true, to_apply=%region_11.0 | all-reduce | flops 4096 | bytes 32768 | tf_op jit(solution)/shard_map/psum | solution.py:31
  121.0 0.6 multiply_add_fusion.1
  121.6 25.7 %reduce-scatter.2.cloned.1.call-done = f32[32,4096]{1,0:T(8,128)} async-done(((f32[256,4096]{1,0:T(8,128)}), f32[32,4096]{1,0:T(8,128)}) %reduce-scatter.2.cloned.1.call-update) | async-done | bytes 524304 | tf_op jit(solution)/shard_map/reduce_scatter | solution.py:40
  (5 shorter events, 0.0 us)
Async XLA Ops:
  7.2 65.8 %copy-start.3 = (bf16[256,256]{1,0:T(8,128)(2,1)S(1)}, bf16[256,256]{1,0:T(8,128)(2,1)}, u32[]{:S(2)}) copy-start(bf16[256,256]{1,0:T(8,128)(2,1)} %param.8) | copy-start | bytes 393220
  7.2 33.4 %all-gather.3.cloned.1.call-start = ((), (), s32[]{:S(2)}) async-start(), calls=%async_computation.1 | async-start | bytes 2359296 | tf_op jit(solution)/shard_map/all_gather | solution.py:16
  7.9 63.0 %all-gather.5.cloned.1.call-start = ((), (), s32[]{:S(2)}) async-start(), calls=%async_computation.2 | async-start | bytes 2359296 | tf_op jit(solution)/shard_map/all_gather | solution.py:18
  10.1 137.2 %reduce-scatter.2.cloned.1.call-start = ((), (), s32[]{:S(2)}) async-start(), calls=%async_computation.3 | async-start | bytes 4718592 | tf_op jit(solution)/shard_map/reduce_scatter | solution.py:40
  40.5 32.5 %copy-start = (bf16[256,4096]{1,0:T(8,128)(2,1)S(1)}, bf16[256,4096]{1,0:T(8,128)(2,1)}, u32[]{:S(2)}) copy-start(bf16[256,4096]{1,0:T(8,128)(2,1)} %all-gather.3.cloned.1.call-done) | copy-start | bytes 6291460
  73.0 3.1 %copy-start.1 = (bf16[256,4096]{1,0:T(8,128)(2,1)S(1)}, bf16[256,4096]{1,0:T(8,128)(2,1)}, u32[]{:S(2)}) copy-start(bf16[256,4096]{1,0:T(8,128)(2,1)} %all-gather.5.cloned.1.call-done) | copy-start | bytes 6291460
  73.0 3.1 %copy-start.2 = (bf16[256,256]{1,0:T(8,128)(2,1)S(1)}, bf16[256,256]{1,0:T(8,128)(2,1)}, u32[]{:S(2)}) copy-start(bf16[256,256]{1,0:T(8,128)(2,1)} %param.7) | copy-start | bytes 393220
  73.0 3.1 %copy-start.4 = (f32[4096]{0:T(1024)S(1)}, f32[4096]{0:T(1024)}, u32[]{:S(2)}) copy-start(f32[4096]{0:T(1024)} %param.9) | copy-start | bytes 49156
Sparse Core Ops, SparseCore 0:
  9.9 30.5 all-gather.2
  43.0 27.8 all-gather.4
  98.7 48.5 reduce-scatter.1
where the time goes:
time: 154 us
  waiting for transfers between devices  82.9 us (54%)
  blocking collectives  34.1 us (22%)
  between operations  13.9 us (9%)
  other arithmetic  13.4 us (9%)
  matrix products  9.39 us (6%)
    all_gather x1, waiting for transfers between devices, shards(): student_full = lax.all_gather(student_weight, 'dp', axis=0, tiled=True)  28.3 us
    all_gather x1, waiting for transfers between devices, shards(): lax.all_gather(master_new.astype(jnp.bfloat16), 'dp', axis=0, tiled=True)  28.2 us
    reduce_scatter x1, waiting for transfers between devices, shards(): lax.psum_scatter((product - student_full.astype(jnp.float32) * scaled) /...  25.7 us
    psum x1, blocking collectives, shards(): cos_mean = lax.psum(jnp.sum(t_cos, 0), 'dp') / images_all  22.4 us
    psum x1, blocking collectives, shards(): lax.psum((jnp.sum(t_exp, 1, keepdims=True), jnp.sum(s_exp, 1, keepdims=Tr...  11.7 us
    reduce_sum x1, other arithmetic, shards(): weighted = jnp.sum(dlog.astype(jnp.float32) * s_cos, 0)  4.47 us
    dot_general x1, matrix products, shards(): raw = jnp.dot(feats, weight, preferred_element_type=jnp.float32)  3.37 us
  transfers between devices with their start and end apart: 3, of which 3 were waited for; matrix products, arithmetic and copies ran while one was open for 5% of the time, Pallas kernels for 0%

commit v1 on v0

--- a/solution.py
+++ b/solution.py
@@ -2,6 +2,18 @@
 import jax.numpy as jnp
 from jax import lax
 from jax.sharding import PartitionSpec as P
+
+
+def doubled_up(shard, axis, dim):
+    ways, here, step = (lax.axis_size(axis), lax.axis_index(axis), shard.shape[dim])
+    line, have = (shard, 1)
+    while have < ways:
+        line = jnp.concatenate(
+            [line, lax.ppermute(line, axis, [(d, (d - have) % ways) for d in range(ways)])],
+            axis=dim,
+        )
+        have = 2 * have
+    return jnp.roll(line, here * step, axis=dim)
 
 
 def unit_rows(feat):
@@ -13,7 +25,7 @@
     zt = unit_rows(teacher_feat)
     zs = unit_rows(student_feat)
     images_all = teacher_feat.shape[0] * lax.axis_size("dp")
-    student_full = lax.all_gather(student_weight, "dp", axis=0, tiled=True)
+    student_full = doubled_up(student_weight, "dp", 0)
     master_new = 0.996 * teacher_master + 0.004 * student_weight.astype(jnp.float32)
     weight = lax.all_gather(master_new.astype(jnp.bfloat16), "dp", axis=0, tiled=True)
     feats = zt

time: 154 us -> 152 us (0.987)
  waiting for transfers between devices: 82.9 us -> 70.6 us
  starting transfers between devices: 0.12 us -> 4.86 us
  local copies, waits for them, and re-layouts: 0.03 us -> 2.73 us
  matrix products: 9.39 us -> 11.1 us
    ppermute x0 -> x3, waiting for transfers between devices: none -> 45 us  [doubled_up(): lax.ppermute(line, axis, [(d, (d - have) % ways) for d in range(ways)])]
    all_gather x1 -> x0, waiting for transfers between devices: 28.3 us -> none  [shards(): student_full = lax.all_gather(student_weight, 'dp', axis=0, tiled=True)]
    all_gather x1, waiting for transfers between devices: 28.2 us -> 0.01 us  [shards(): lax.all_gather(master_new.astype(jnp.bfloat16), 'dp', axis=0, tiled=True)]
    ppermute x0 -> x3, starting transfers between devices: none -> 4.79 us  [doubled_up(): lax.ppermute(line, axis, [(d, (d - have) % ways) for d in range(ways)])]
    unnamed x10 -> x19, local copies, waits for them, and re-layouts: 0.03 us -> 2.65 us
    concatenate x0 -> x2, other arithmetic: none -> 2.02 us  [doubled_up(): jnp.concatenate([line, lax.ppermute(line, axis, [(d, (d - have) % ways) f...]
    reduce_sum x1, other arithmetic: 2.18 us -> 0.45 us  [shards(): jnp.sum(jnp.square(student_full.astype(jnp.float32)), 0) + 1e-06]
    dot_general x1, matrix products: 3.37 us -> 4.94 us  [shards(): raw = jnp.dot(feats, weight, preferred_element_type=jnp.float32)]
  transfers between devices with their start and end apart: 3 -> 5, of which waited for: 3 -> 4; matrix products, arithmetic and copies ran while one was open for 5% -> 8% of each run, Pallas kernels for 0% -> 0%
where the time goes in v1:
time: 152 us
  waiting for transfers between devices  70.6 us (46%)
  blocking collectives  34.3 us (23%)
  between operations  14.2 us (9%)
  other arithmetic  13.9 us (9%)
  matrix products  11.1 us (7%)
  starting transfers between devices  4.86 us (3%)
  local copies, waits for them, and re-layouts  2.73 us (2%)
    ppermute x3, waiting for transfers between devices, doubled_up(): lax.ppermute(line, axis, [(d, (d - have) % ways) for d in range(ways)])  45 us
    reduce_scatter x1, waiting for transfers between devices, shards(): lax.psum_scatter((product - student_full.astype(jnp.float32) * scaled) /...  25.6 us
    psum x1, blocking collectives, shards(): cos_mean = lax.psum(jnp.sum(t_cos, 0), 'dp') / images_all  22.4 us
    psum x1, blocking collectives, shards(): lax.psum((jnp.sum(t_exp, 1, keepdims=True), jnp.sum(s_exp, 1, keepdims=Tr...  11.9 us
    dot_general x1, matrix products, shards(): raw = jnp.dot(feats, weight, preferred_element_type=jnp.float32)  4.94 us
    ppermute x3, starting transfers between devices, doubled_up(): lax.ppermute(line, axis, [(d, (d - have) % ways) for d in range(ways)])  4.79 us
    reduce_sum x1, other arithmetic, shards(): weighted = jnp.sum(dlog.astype(jnp.float32) * s_cos, 0)  4.61 us
    dot_general x1, matrix products, shards(): jnp.dot(zs, student_full, preferred_element_type=jnp.float32) / s_norm  3.13 us
  transfers between devices with their start and end apart: 5, of which 4 were waited for; matrix products, arithmetic and copies ran while one was open for 8% of the time, Pallas kernels for 0%

profile of v1, /device:TPU:0, one launch (start us, length us, event | category | flops | bytes accessed | tf_op | source)
XLA Modules:
  0.0 151.7 jit_solution(2176392929709355145)
XLA Ops:
  7.2 0.0 all-gather.2.cloned.1.call-start
  7.2 3.4 %collective-permute-start = (bf16[32,4096]{1,0:T(8,128)(2,1)}, bf16[32,4096]{1,0:T(8,128)(2,1)S(1)}, u32[]{:S(2)}, u32[]{:S(2)}) collective-permute-start(bf16[32,4096]{1,0:T(8,128)(2,1)} %param.6), channel_id=1, source_target_pairs={{0,28},{4,0},{8,4},{12,8},{16,12},{20,16},{24,20},{28,24},{1,29},{... | collective-permute-start | bytes 786440 | tf_op jit(solution)/shard_map/ppermute | solution.py:12
  10.6 2.1 %fusion.19 = (bf16[32,4096]{1,0:T(8,128)(2,1)}, f32[32,4096]{1,0:T(8,128)}) fusion(bf16[32,4096]{1,0:T(8,128)(2,1)} %param.6, f32[32,4096]{1,0:T(8,128)} %param.5), kind=kLoop, calls=%fused_computation.44 | loop fusion | flops 655360 | bytes 1572864 | tf_op jit(solution)/shard_map/convert_element_type | solution.py:30
  12.7 0.0 all-gather.2.cloned.1.call-update
  12.7 0.0 reduce-scatter.2.cloned.1.call-start
  12.7 1.0 fusion.8
  13.8 1.0 collective-permute-done
  14.8 1.0 pad_maximum_fusion.1
  15.8 0.6 collective-permute-start.1
  16.4 1.0 fusion.6
  17.4 1.0 constant_dynamic-update-slice_fusion.7
  18.4 14.5 %collective-permute-done.1 = bf16[64,4096]{1,0:T(8,128)(2,1)S(1)} collective-permute-done((bf16[64,4096]{1,0:T(8,128)(2,1)S(1)}, bf16[64,4096]{1,0:T(8,128)(2,1)S(1)}, u32[]{:S(2)}, u32[]{:S(2)}) %collective-permute-start.1) | collective-permute-done | bytes 524320 | tf_op jit(solution)/shard_map/ppermute | solution.py:12
  32.9 1.0 pad_maximum_fusion
  33.9 0.8 collective-permute-start.2
  34.8 0.0 copy-start.4
  34.8 29.5 %collective-permute-done.2 = bf16[128,4096]{1,0:T(8,128)(2,1)S(1)} collective-permute-done((bf16[128,4096]{1,0:T(8,128)(2,1)S(1)}, bf16[128,4096]{1,0:T(8,128)(2,1)S(1)}, u32[]{:S(2)}, u32[]{:S(2)}) %collective-permute-start.2) | collective-permute-done | bytes 1048608 | tf_op jit(solution)/shard_map/ppermute | solution.py:12
  64.3 0.1 constant_dynamic-update-slice_fusion.4
  64.5 0.1 constant_dynamic-update-slice_fusion
  64.6 0.4 fusion
  65.0 1.4 copy-done.1
  66.5 0.0 copy-done.4
  66.5 3.1 %fusion.3 = (f32[256]{0:T(256)S(1)}, f32[256,4096]{1,0:T(8,128)}) fusion(f32[4096]{0:T(1024)S(1)} %add_sqrt_fusion.1, bf16[512,4096]{1,0:T(8,128)(2,1)S(1)} %constant_dynamic-update-slice_fusion, s32[]{:T(128)S(6)} %select_n.14, bf16[256,256]{1,0:T(8,128)(2,1)S(1)} %copy-done.4, f32[256]{0:T(256)S(1)} %add_rsqrt_fusion.1), kind=kOutput, calls=%fused_computation.12 | convolution fusion | flops 540212992 | bytes 6440964 | tf_op jit(solution)/shard_map/dot_general | solution.py:37
  69.6 2.0 %multiply_reduce_fusion.1 = f32[4096]{0:T(1024)S(1)} fusion(bf16[256,4096]{1,0:T(8,128)(2,1)} %all-gather.2.cloned.1.call-done), kind=kLoop, calls=%fused_computation.10 | loop fusion | flops 3141632 | bytes 2113536 | tf_op jit(solution)/shard_map/reduce_sum | solution.py:33
  71.7 4.9 %fusion.18 = (f32[4096]{0:T(1024)S(1)}, f32[256]{0:T(256)S(1)}, f32[256,4096]{1,0:T(8,128)}) fusion(f32[4096]{0:T(1024)S(1)} %copy-done.5, f32[4096]{0:T(1024)S(1)} %add_sqrt_fusion, bf16[256,4096]{1,0:T(8,128)(2,1)} %all-gather.2.cloned.1.call-done, bf16[256,256]{1,0:T(8,128)(2,1)S(1)} %copy-done.3, f32[256]{0:T(256)S(1)} %add_rsqrt_fusion), kind=kOutput, calls=%fused_computation.43 | convolution fusion | flops 542306048 | bytes 6473728 | tf_op jit(solution)/shard_map/dot_general | solution.py:32
  76.6 11.9 %all-reduce = (f32[256]{0:T(256)S(1)}, f32[256]{0:T(256)S(1)}) all-reduce(f32[256]{0:T(256)S(1)} %get-tuple-element.4, f32[256]{0:T(256)S(1)} %get-tuple-element.12), channel_id=1, replica_groups=mesh['dp'=8,'tensor'=4] {'tensor'}, use_global_device_ids=true, to_apply=%region_7.8 | all-reduce | flops 512 | bytes 4096 | tf_op jit(solution)/shard_map/psum | solution.py:40
  88.6 4.6 %multiply_reduce_fusion = (f32[4096]{0:T(1024)S(1)}, bf16[256,4096]{1,0:T(8,128)(2,1)S(1)}) fusion(f32[256,4096]{1,0:T(8,128)} %get-tuple-element.13, f32[256]{0:T(256)S(1)} %get-tuple-element.5, f32[256,4096]{1,0:T(8,128)} %get-tuple-element.11, f32[4096]{0:T(1024)S(1)} %copy-done.5, f32[256]{0:T(256)S(1)} %get-tuple-element.6), kind=kLoop, calls=%fused_computation.7 | loop fusion | flops 11530240 | bytes 10520576 | tf_op jit(solution)/shard_map/reduce_sum | solution.py:46
  93.2 0.0 copy-done.2
  93.2 3.0 %fusion.2 = f32[256,4096]{1,0:T(8,128)} fusion(f32[4096]{0:T(1024)S(1)} %rsqrt_multiply_fusion, f32[4096]{0:T(1024)S(1)} %add_sqrt_fusion.1, bf16[512,4096]{1,0:T(8,128)(2,1)S(1)} %copy-done.2, s32[]{:T(128)S(6)} %select_n.14, bf16[256,4096]{1,0:T(8,128)(2,1)S(1)} %get-tuple-element.8, bf16[256,256]{1,0:T(8,128)(2,1)S(1)} %copy-done.4, ...), kind=kOutput, calls=%fused_computation.6 | convolution fusion | flops 541261824 | bytes 8553476 | tf_op jit(solution)/shard_map/dot_general | solution.py:49
  96.2 0.0 reduce-scatter.2.cloned.1.call-update
  96.2 22.4 %psum.23 = f32[4096]{0:T(1024)S(1)} all-reduce(f32[4096]{0:T(1024)S(1)} %get-tuple-element.3), channel_id=1, replica_groups=mesh['dp'=8,'tensor'=4] {'dp'}, use_global_device_ids=true, to_apply=%region_11.12 | all-reduce | flops 4096 | bytes 32768 | tf_op jit(solution)/shard_map/psum | solution.py:43
  118.6 0.6 multiply_add_fusion.1
  119.3 25.6 %reduce-scatter.2.cloned.1.call-done = f32[32,4096]{1,0:T(8,128)} async-done(((f32[256,4096]{1,0:T(8,128)}), f32[32,4096]{1,0:T(8,128)}) %reduce-scatter.2.cloned.1.call-update) | async-done | bytes 524304 | tf_op jit(solution)/shard_map/reduce_scatter | solution.py:52
  (19 shorter events, 0.2 us)
Async XLA Ops:
  7.2 62.5 %all-gather.2.cloned.1.call-start = ((), (), s32[]{:S(2)}) async-start(), calls=%async_computation.1 | async-start | bytes 2359296 | tf_op jit(solution)/shard_map/all_gather | solution.py:30
  7.2 7.6 %collective-permute-start = (bf16[32,4096]{1,0:T(8,128)(2,1)}, bf16[32,4096]{1,0:T(8,128)(2,1)S(1)}, u32[]{:S(2)}, u32[]{:S(2)}) collective-permute-start(bf16[32,4096]{1,0:T(8,128)(2,1)} %param.6), channel_id=1, source_target_pairs={{0,28},{4,0},{8,4},{12,8},{16,12},{20,16},{24,20},{28,24},{1,29},{... | collective-permute-start | bytes 786440 | tf_op jit(solution)/shard_map/ppermute | solution.py:12
  12.7 51.7 %copy-start = (bf16[32,4096]{1,0:T(8,128)(2,1)S(1)}, bf16[32,4096]{1,0:T(8,128)(2,1)}, u32[]{:S(2)}) copy-start(bf16[32,4096]{1,0:T(8,128)(2,1)} %param.6) | copy-start | bytes 786436
  12.7 132.2 %reduce-scatter.2.cloned.1.call-start = ((), (), s32[]{:S(2)}) async-start(), calls=%async_computation.2 | async-start | bytes 4718592 | tf_op jit(solution)/shard_map/reduce_scatter | solution.py:52
  15.8 17.1 %collective-permute-start.1 = (bf16[64,4096]{1,0:T(8,128)(2,1)S(1)}, bf16[64,4096]{1,0:T(8,128)(2,1)S(1)}, u32[]{:S(2)}, u32[]{:S(2)}) collective-permute-start(bf16[64,4096]{1,0:T(8,128)(2,1)S(1)} %pad_maximum_fusion.1), channel_id=1, source_target_pairs={{0,24},{4,28},{8,0},{12,4},{16,8},{20,12},{24,16},{28,20},{1,25},{... | collective-permute-start | bytes 1572872 | tf_op jit(solution)/shard_map/ppermute | solution.py:12
  33.9 30.4 %collective-permute-start.2 = (bf16[128,4096]{1,0:T(8,128)(2,1)S(1)}, bf16[128,4096]{1,0:T(8,128)(2,1)S(1)}, u32[]{:S(2)}, u32[]{:S(2)}) collective-permute-start(bf16[128,4096]{1,0:T(8,128)(2,1)S(1)} %pad_maximum_fusion), channel_id=1, source_target_pairs={{0,16},{4,20},{8,24},{12,28},{16,0},{20,4},{24,8},{28,12},{1,17},{... | collective-permute-start | bytes 3145736 | tf_op jit(solution)/shard_map/ppermute | solution.py:12
  34.8 31.7 %copy-start.4 = (bf16[256,256]{1,0:T(8,128)(2,1)S(1)}, bf16[256,256]{1,0:T(8,128)(2,1)}, u32[]{:S(2)}) copy-start(bf16[256,256]{1,0:T(8,128)(2,1)} %param.8) | copy-start | bytes 393220
  64.6 1.9 %copy-start.1 = (bf16[512,4096]{1,0:T(8,128)(2,1)}, bf16[512,4096]{1,0:T(8,128)(2,1)S(1)}, u32[]{:S(2)}) copy-start(bf16[512,4096]{1,0:T(8,128)(2,1)S(1)} %constant_dynamic-update-slice_fusion) | copy-start | bytes 12582916
  66.5 5.2 %copy-start.3 = (bf16[256,256]{1,0:T(8,128)(2,1)S(1)}, bf16[256,256]{1,0:T(8,128)(2,1)}, u32[]{:S(2)}) copy-start(bf16[256,256]{1,0:T(8,128)(2,1)} %param.7) | copy-start | bytes 393220
  66.5 5.2 %copy-start.5 = (f32[4096]{0:T(1024)S(1)}, f32[4096]{0:T(1024)}, u32[]{:S(2)}) copy-start(f32[4096]{0:T(1024)} %param.9) | copy-start | bytes 49156
  88.6 4.7 %copy-start.2 = (bf16[512,4096]{1,0:T(8,128)(2,1)S(1)}, bf16[512,4096]{1,0:T(8,128)(2,1)}, u32[]{:S(2)}) copy-start(bf16[512,4096]{1,0:T(8,128)(2,1)} %copy-done.1) | copy-start | bytes 12582916
Sparse Core Ops, SparseCore 0:
  12.8 38.3 all-gather.1
  96.4 48.4 reduce-scatter.1
